TPU v7x, 256 devices: a whole 4x4x8 slice. The times are simulated.
256 devices in a mesh: req: 16 (over x, y), cuts: 16 (over z, core).
Axes of the slice: x: 4, y: 4, z: 8, core: 2. Of those that a mesh axis runs over, the one named last changes fastest.
Arguments:
- queries: bfloat16 [16, 2048, 1024], P('req', 'cuts')
- new_keys: bfloat16 [16, 2048, 1024], P('req', 'cuts'), may hold values from -6 to 6
- new_values: bfloat16 [16, 2048, 1024], P('req', 'cuts'), may hold values from -12 to 12
- cache_keys: bfloat16 [16, 4096, 1024], P('req', 'cuts')
- cache_values: bfloat16 [16, 4096, 1024], P('req', 'cuts'), may hold values from -12 to 12
- cache_lengths: int32 [16], P('req'), may hold values from 2 to 4096, as said below
- relative_bias: float32 [16, 32], replicated, may hold values from -4 to 4
- residual: bfloat16 [16, 2048, 1024], P('req', 'cuts')
- out_weight: bfloat16 [1024, 1024], replicated, may hold values from -0.1875 to 0.1875
- norm_gain: bfloat16 [1024], replicated, may hold values from 0.5 to 1.5
- router_weight: bfloat16 [1024, 16], replicated, may hold values from -0.1875 to 0.1875
- routes: int32 [16, 2048, 2], P('req', 'cuts'), may hold values from 0 to 15, all different within a row; in each aligned block of 128 rows (0 to 127, 128 to 255, ..., all dimensions but the last counted through in order) at most 20 rows name the same one
- gate_weight: bfloat16 [16, 1024, 2816], P('req', None, 'cuts'), may hold values from -0.1875 to 0.1875
- up_weight: bfloat16 [16, 1024, 2816], P('req', None, 'cuts'), may hold values from -0.1875 to 0.1875
- down_weight: bfloat16 [16, 1024, 2816], P('req', None, 'cuts'), may hold values from -0.109375 to 0.109375
Outputs:
- layer_out: bfloat16 [16, 2048, 1024], P('req', 'cuts')
Inputs may be any that keep to these rules, and one draw needn't show every extreme that they name: `cache_lengths`: each cached length lies under 256 or above 3840; some request's cache is full. `routes`: among the 128 tokens of one device no expert is named by more than 20 tokens, a bound that some block reaches.
All inputs are finite; a program needn't handle non-finite values.
Results may differ from a plain program's by a relative error of at most 0.03.
Values may be sent and summed in bfloat16 or wider, within the bound.
No kernel may reach another device: no remote copies, remote signals or barrier semaphores. Data moves between devices by JAX's collectives and lax.ppermute only.
A program may use at most 128 MiB of HBM per device.

v0:
```python
from functools import partial
import jax
import jax.numpy as jnp
import numpy as np
from jax import lax
from jax.sharding import PartitionSpec as P

MAXDIST = 128


def shortened(value):
    return jax.tree.map(lambda a: a.astype(jnp.bfloat16) if a.dtype == jnp.float32 else a, value)


def bucket_number(distance, bucket_count, reach_limit):
    exact_count = bucket_count // 2
    if distance < exact_count:
        return distance
    level_value = exact_count + int(
        np.floor(exact_count * np.log(distance / exact_count) / np.log(reach_limit / exact_count))
    )
    return min(bucket_count - 1, level_value)


def bucket_edges(bucket_count, reach_limit):
    edge_list = []
    for target in range(1, bucket_count):
        probe_value = 0
        while bucket_number(probe_value, bucket_count, reach_limit) < target:
            probe_value += 1
        edge_list.append(probe_value)
    return edge_list


def bucket_index(distance, edge_list):
    bucket_level = jnp.zeros(distance.shape, jnp.int32)
    for edge_value in edge_list:
        bucket_level = bucket_level + (distance >= edge_value).astype(jnp.int32)
    return bucket_level


def block_masks(block_index, length, cache_rows, q_rows, query_total, bucket_count):
    cache_slots = block_index * cache_rows + jnp.arange(cache_rows, dtype=jnp.int32)
    new_slots = block_index * q_rows + jnp.arange(q_rows, dtype=jnp.int32)
    key_pos = jnp.concatenate([cache_slots, length + new_slots])
    key_live = jnp.concatenate([cache_slots < length, new_slots >= 0])
    query_pos = length + jnp.arange(query_total, dtype=jnp.int32)
    visible = key_live[None, :] & (key_pos[None, :] <= query_pos[:, None])
    distance = jnp.maximum(query_pos[:, None] - key_pos[None, :], 0)
    return (visible, bucket_index(distance, bucket_edges(bucket_count, MAXDIST)))


def head_partial(visible, bucket, operands):
    query_rows, key_rows, value_rows, bias_table = operands
    scores = (
        lax.dot_general(
            query_rows, key_rows, (((1,), (1,)), ((), ())), preferred_element_type=jnp.float32
        )
        / 8.0
    )
    masked = jnp.where(visible, scores + jnp.take(bias_table, bucket), -1e30)
    block_peak = jnp.max(masked, axis=1)
    weights = jnp.where(visible, jnp.exp(masked - block_peak[:, None]), 0.0)
    block_total = jnp.sum(weights, axis=1)
    numerator = jnp.dot(
        weights.astype(jnp.bfloat16), value_rows, preferred_element_type=jnp.float32
    )
    block_out = (numerator / jnp.maximum(block_total, 1.0)[:, None]).astype(jnp.bfloat16)
    return (block_out, block_peak, block_total)


def block_partials(query_rows, key_rows, value_rows, tables, visible, bucket):
    head_count = tables.shape[0]
    head_dim = query_rows.shape[1] // head_count
    head_queries = query_rows.reshape(query_rows.shape[0], head_count, head_dim).transpose(1, 0, 2)
    head_keys = key_rows.reshape(key_rows.shape[0], head_count, head_dim).transpose(1, 0, 2)
    head_values = value_rows.reshape(value_rows.shape[0], head_count, head_dim).transpose(1, 0, 2)
    return lax.map(
        partial(head_partial, visible, bucket), (head_queries, head_keys, head_values, tables)
    )


def merge_blocks(block_out, block_peak, block_total):
    best_peak = jnp.max(block_peak, axis=0)
    factor = jnp.exp(block_peak - best_peak[None]) * block_total
    weighted = jnp.sum(factor[..., None] * block_out.astype(jnp.float32), axis=0)
    return (weighted / jnp.sum(factor, axis=0)[..., None]).astype(jnp.bfloat16)


def expert_part(row_block, gate_piece, up_piece, down_piece):
    gate_act = jnp.einsum(
        "necd,edf->necf", row_block, gate_piece, preferred_element_type=jnp.float32
    )
    up_act = jnp.einsum("necd,edf->necf", row_block, up_piece, preferred_element_type=jnp.float32)
    act_rows = (jax.nn.gelu(gate_act) * up_act).astype(jnp.bfloat16)
    return jnp.einsum("necf,edf->necd", act_rows, down_piece, preferred_element_type=jnp.float32)


def per_device(
    queries,
    new_keys,
    new_values,
    cache_keys,
    cache_values,
    cache_lengths,
    relative_bias,
    residual,
    out_weight,
    norm_gain,
    router_weight,
    routes,
    gate_weight,
    up_weight,
    down_weight,
):
    cut_count = lax.axis_size("cuts")
    cut_index = lax.axis_index("cuts")
    q_rows = queries.shape[1]
    cache_rows = cache_keys.shape[1]
    model_width = queries.shape[2]
    head_count = relative_bias.shape[0]
    head_dim = model_width // head_count
    bucket_count = relative_bias.shape[1]
    length = cache_lengths[0]
    query_total = q_rows * cut_count
    local_keys = jnp.concatenate([cache_keys[0], new_keys[0]], axis=0)
    local_values = jnp.concatenate([cache_values[0], new_values[0]], axis=0)
    every_query = lax.all_gather(queries[0], "cuts", axis=0, tiled=True)
    visible, bucket = block_masks(cut_index, length, cache_rows, q_rows, query_total, bucket_count)
    block_out, block_peak, block_total = block_partials(
        every_query, local_keys, local_values, relative_bias, visible, bucket
    )
    block_out = block_out.transpose(1, 0, 2).reshape(cut_count, q_rows, model_width)
    block_peak = block_peak.T.reshape(cut_count, q_rows, head_count)
    block_total = block_total.T.reshape(cut_count, q_rows, head_count)
    block_out = lax.all_to_all(
        shortened(block_out), "cuts", split_axis=0, concat_axis=0, tiled=True
    ).astype(block_out.dtype)
    block_peak, block_total = (
        lax.all_to_all(
            shortened(block_peak), "cuts", split_axis=0, concat_axis=0, tiled=True
        ).astype(block_peak.dtype),
        lax.all_to_all(
            shortened(block_total), "cuts", split_axis=0, concat_axis=0, tiled=True
        ).astype(block_total.dtype),
    )
    block_out = block_out.reshape(cut_count, q_rows, head_count, head_dim)
    attended = merge_blocks(block_out, block_peak, block_total).reshape(q_rows, model_width)
    hidden = residual[0].astype(jnp.float32) + jnp.dot(
        attended, out_weight, preferred_element_type=jnp.float32
    )
    inv_rms = lax.rsqrt(jnp.mean(hidden * hidden, axis=1, keepdims=True) + 1e-06)
    normed = (hidden * inv_rms * norm_gain.astype(jnp.float32)).astype(jnp.bfloat16)
    experts = router_weight.shape[1]
    capacity = (10 * q_rows + 4 * experts - 1) // (4 * experts)
    logits = jnp.dot(normed, router_weight, preferred_element_type=jnp.float32)
    chosen = routes[0]
    onehot = (chosen[:, :, None] == jnp.arange(experts, dtype=jnp.int32)[None, None, :]).astype(
        jnp.float32
    )
    gate_values = jax.nn.sigmoid(jnp.sum(onehot * logits[:, None, :], axis=2))
    named_count = jnp.sum(onehot, axis=1)
    earlier_mask = (jnp.arange(q_rows)[:, None] > jnp.arange(q_rows)[None, :]).astype(jnp.bfloat16)
    earlier = jnp.dot(
        earlier_mask, named_count.astype(jnp.bfloat16), preferred_element_type=jnp.float32
    )
    slot_number = jnp.sum(onehot * earlier[:, None, :], axis=2)
    slot_hot = (
        slot_number[:, :, None] == jnp.arange(capacity, dtype=jnp.float32)[None, None, :]
    ).astype(jnp.float32)
    dispatch = jnp.einsum("tke,tkc->ect", onehot, slot_hot)
    buffers = jnp.einsum(
        "ect,td->ecd", dispatch.astype(jnp.bfloat16), normed, preferred_element_type=jnp.float32
    ).astype(jnp.bfloat16)
    arrived = lax.all_to_all(buffers, "req", split_axis=0, concat_axis=0, tiled=True)
    local_experts = gate_weight.shape[0]
    gathered = lax.all_gather(arrived, "cuts", axis=0, tiled=True)
    row_count = lax.axis_size("cuts") * arrived.shape[0]
    row_block = gathered.reshape(row_count, local_experts, capacity, model_width)
    expert_out = lax.psum_scatter(
        expert_part(row_block, gate_weight, up_weight, down_weight)
        .reshape(row_count, local_experts * capacity, model_width)
        .astype(jnp.bfloat16),
        "cuts",
        scatter_dimension=0,
        tiled=True,
    )
    returned = lax.all_to_all(expert_out, "req", split_axis=0, concat_axis=0, tiled=True)
    combine = jnp.einsum(
        "tke,tkc,tk->ect", onehot, slot_hot, gate_values, precision=lax.Precision.HIGHEST
    )
    gathered_back = jnp.einsum(
        "ect,ecd->td", combine, returned.astype(jnp.float32), precision=lax.Precision.HIGHEST
    )
    layer_out = hidden + gathered_back
    return layer_out.astype(jnp.bfloat16)[None]


def solution(mesh):
    return jax.shard_map(
        per_device,
        mesh=mesh,
        in_specs=(
            P("req", "cuts", None),
            P("req", "cuts", None),
            P("req", "cuts", None),
            P("req", "cuts", None),
            P("req", "cuts", None),
            P("req"),
            P(),
            P("req", "cuts", None),
            P(),
            P(),
            P(),
            P("req", "cuts", None),
            P("req", None, "cuts"),
            P("req", None, "cuts"),
            P("req", None, "cuts"),
        ),
        out_specs=P("req", "cuts", None),
        check_vma=False,
    )
```

profile of v0, /device:TPU:97, one launch (start us, length us, event | category | flops | bytes accessed | tf_op | source)
XLA Modules:
  0.0 969.2 jit_solution(8223163654308807281)
XLA Ops:
  17.1 10.8 %convert_add_fusion = s32[2048,384]{0,1:T(8,128)} fusion(s32[384]{0:T(512)S(1)} %pad_add_fusion, s32[2048]{0:T(1024)S(1)} %iota_add_fusion), kind=kLoop, calls=%fused_computation.63 | loop fusion | flops 73924608 | bytes 3155456 | tf_op jit(solution)/shard_map/add | solution.py:38
  27.9 31.0 %all-gather.6.cloned.1.call-done = bf16[1,2048,1024]{1,2,0:T(8,128)(2,1)} async-done(((bf16[1,128,1024]{1,2,0:T(8,128)(2,1)}), bf16[1,2048,1024]{1,2,0:T(8,128)(2,1)}) %all-gather.6.cloned.1.call-update) | async-done | bytes 4194320 | tf_op jit(solution)/shard_map/all_gather | solution.py:128
  58.9 562.9 %while.15 = (s32[]{:T(128)}, bf16[16,2048,64]{1,2,0:T(8,128)(2,1)}, bf16[16,2048]{1,0:T(8,128)(2,1)S(1)}, bf16[16,2048]{1,0:T(8,128)(2,1)S(1)}, bf16[16,2048,64]...) while((s32[]{:T(128)}, bf16[16,2048,64]{1,2,0:T(8,128)(2,1)}, ...), condition=%wide.region_3.4_spmd.clone, body=%wide.region_0.3_spmd.clone.sunk | while | flops 270792704 | bytes 13345049 | solution.py:78
  61.0 29.3 %fusion.139 = (f32[2048]{0:T(1024)S(1)}, f32[2048,384]{0,1:T(8,128)S(1)}) fusion(f32[]{:T(128)} %bitcast.298, f32[]{:T(128)} %bitcast.299, f32[]{:T(128)} %bitcast.300, f32[]{:T(128)} %bitcast.301, f32[]{:T(128)} %bitcast.302, f32[]{:T(128)} %bitcast.303, f32[]{:T(128)} %bitcast.304, f32[]{:T(128)} %bitcast.305, f32[]{:T(128)} %bitcast.306, ...), kind=kOutput, calls=%fused_computation.158.clone.1 | convolution fusion | flops 162002944 | bytes 6638464 | tf_op jit(solution)/shard_map/while/body/eval_jaxpr/dot_general | solution.py:56
  96.2 29.3 %fusion.139 = (f32[2048]{0:T(1024)S(1)}, f32[2048,384]{0,1:T(8,128)S(1)}) fusion(f32[]{:T(128)} %bitcast.298, f32[]{:T(128)} %bitcast.299, f32[]{:T(128)} %bitcast.300, f32[]{:T(128)} %bitcast.301, f32[]{:T(128)} %bitcast.302, f32[]{:T(128)} %bitcast.303, f32[]{:T(128)} %bitcast.304, f32[]{:T(128)} %bitcast.305, f32[]{:T(128)} %bitcast.306, ...), kind=kOutput, calls=%fused_computation.158.clone.1 | convolution fusion | flops 162002944 | bytes 6638464 | tf_op jit(solution)/shard_map/while/body/eval_jaxpr/dot_general | solution.py:56
  126.5 2.6 fusion.141
  131.4 29.3 %fusion.139 = (f32[2048]{0:T(1024)S(1)}, f32[2048,384]{0,1:T(8,128)S(1)}) fusion(f32[]{:T(128)} %bitcast.298, f32[]{:T(128)} %bitcast.299, f32[]{:T(128)} %bitcast.300, f32[]{:T(128)} %bitcast.301, f32[]{:T(128)} %bitcast.302, f32[]{:T(128)} %bitcast.303, f32[]{:T(128)} %bitcast.304, f32[]{:T(128)} %bitcast.305, f32[]{:T(128)} %bitcast.306, ...), kind=kOutput, calls=%fused_computation.158.clone.1 | convolution fusion | flops 162002944 | bytes 6638464 | tf_op jit(solution)/shard_map/while/body/eval_jaxpr/dot_general | solution.py:56
  161.7 2.5 fusion.141
  166.6 29.3 %fusion.139 = (f32[2048]{0:T(1024)S(1)}, f32[2048,384]{0,1:T(8,128)S(1)}) fusion(f32[]{:T(128)} %bitcast.298, f32[]{:T(128)} %bitcast.299, f32[]{:T(128)} %bitcast.300, f32[]{:T(128)} %bitcast.301, f32[]{:T(128)} %bitcast.302, f32[]{:T(128)} %bitcast.303, f32[]{:T(128)} %bitcast.304, f32[]{:T(128)} %bitcast.305, f32[]{:T(128)} %bitcast.306, ...), kind=kOutput, calls=%fused_computation.158.clone.1 | convolution fusion | flops 162002944 | bytes 6638464 | tf_op jit(solution)/shard_map/while/body/eval_jaxpr/dot_general | solution.py:56
  196.9 2.5 fusion.141
  201.8 29.3 %fusion.139 = (f32[2048]{0:T(1024)S(1)}, f32[2048,384]{0,1:T(8,128)S(1)}) fusion(f32[]{:T(128)} %bitcast.298, f32[]{:T(128)} %bitcast.299, f32[]{:T(128)} %bitcast.300, f32[]{:T(128)} %bitcast.301, f32[]{:T(128)} %bitcast.302, f32[]{:T(128)} %bitcast.303, f32[]{:T(128)} %bitcast.304, f32[]{:T(128)} %bitcast.305, f32[]{:T(128)} %bitcast.306, ...), kind=kOutput, calls=%fused_computation.158.clone.1 | convolution fusion | flops 162002944 | bytes 6638464 | tf_op jit(solution)/shard_map/while/body/eval_jaxpr/dot_general | solution.py:56
  236.9 29.3 %fusion.139 = (f32[2048]{0:T(1024)S(1)}, f32[2048,384]{0,1:T(8,128)S(1)}) fusion(f32[]{:T(128)} %bitcast.298, f32[]{:T(128)} %bitcast.299, f32[]{:T(128)} %bitcast.300, f32[]{:T(128)} %bitcast.301, f32[]{:T(128)} %bitcast.302, f32[]{:T(128)} %bitcast.303, f32[]{:T(128)} %bitcast.304, f32[]{:T(128)} %bitcast.305, f32[]{:T(128)} %bitcast.306, ...), kind=kOutput, calls=%fused_computation.158.clone.1 | convolution fusion | flops 162002944 | bytes 6638464 | tf_op jit(solution)/shard_map/while/body/eval_jaxpr/dot_general | solution.py:56
  267.2 2.6 fusion.141
  272.1 29.3 %fusion.139 = (f32[2048]{0:T(1024)S(1)}, f32[2048,384]{0,1:T(8,128)S(1)}) fusion(f32[]{:T(128)} %bitcast.298, f32[]{:T(128)} %bitcast.299, f32[]{:T(128)} %bitcast.300, f32[]{:T(128)} %bitcast.301, f32[]{:T(128)} %bitcast.302, f32[]{:T(128)} %bitcast.303, f32[]{:T(128)} %bitcast.304, f32[]{:T(128)} %bitcast.305, f32[]{:T(128)} %bitcast.306, ...), kind=kOutput, calls=%fused_computation.158.clone.1 | convolution fusion | flops 162002944 | bytes 6638464 | tf_op jit(solution)/shard_map/while/body/eval_jaxpr/dot_general | solution.py:56
  302.4 2.5 fusion.141
  307.3 29.3 %fusion.139 = (f32[2048]{0:T(1024)S(1)}, f32[2048,384]{0,1:T(8,128)S(1)}) fusion(f32[]{:T(128)} %bitcast.298, f32[]{:T(128)} %bitcast.299, f32[]{:T(128)} %bitcast.300, f32[]{:T(128)} %bitcast.301, f32[]{:T(128)} %bitcast.302, f32[]{:T(128)} %bitcast.303, f32[]{:T(128)} %bitcast.304, f32[]{:T(128)} %bitcast.305, f32[]{:T(128)} %bitcast.306, ...), kind=kOutput, calls=%fused_computation.158.clone.1 | convolution fusion | flops 162002944 | bytes 6638464 | tf_op jit(solution)/shard_map/while/body/eval_jaxpr/dot_general | solution.py:56
  342.5 29.3 %fusion.139 = (f32[2048]{0:T(1024)S(1)}, f32[2048,384]{0,1:T(8,128)S(1)}) fusion(f32[]{:T(128)} %bitcast.298, f32[]{:T(128)} %bitcast.299, f32[]{:T(128)} %bitcast.300, f32[]{:T(128)} %bitcast.301, f32[]{:T(128)} %bitcast.302, f32[]{:T(128)} %bitcast.303, f32[]{:T(128)} %bitcast.304, f32[]{:T(128)} %bitcast.305, f32[]{:T(128)} %bitcast.306, ...), kind=kOutput, calls=%fused_computation.158.clone.1 | convolution fusion | flops 162002944 | bytes 6638464 | tf_op jit(solution)/shard_map/while/body/eval_jaxpr/dot_general | solution.py:56
  372.8 2.5 fusion.141
  377.7 29.3 %fusion.139 = (f32[2048]{0:T(1024)S(1)}, f32[2048,384]{0,1:T(8,128)S(1)}) fusion(f32[]{:T(128)} %bitcast.298, f32[]{:T(128)} %bitcast.299, f32[]{:T(128)} %bitcast.300, f32[]{:T(128)} %bitcast.301, f32[]{:T(128)} %bitcast.302, f32[]{:T(128)} %bitcast.303, f32[]{:T(128)} %bitcast.304, f32[]{:T(128)} %bitcast.305, f32[]{:T(128)} %bitcast.306, ...), kind=kOutput, calls=%fused_computation.158.clone.1 | convolution fusion | flops 162002944 | bytes 6638464 | tf_op jit(solution)/shard_map/while/body/eval_jaxpr/dot_general | solution.py:56
  408.0 2.5 fusion.141
  412.8 29.3 %fusion.139 = (f32[2048]{0:T(1024)S(1)}, f32[2048,384]{0,1:T(8,128)S(1)}) fusion(f32[]{:T(128)} %bitcast.298, f32[]{:T(128)} %bitcast.299, f32[]{:T(128)} %bitcast.300, f32[]{:T(128)} %bitcast.301, f32[]{:T(128)} %bitcast.302, f32[]{:T(128)} %bitcast.303, f32[]{:T(128)} %bitcast.304, f32[]{:T(128)} %bitcast.305, f32[]{:T(128)} %bitcast.306, ...), kind=kOutput, calls=%fused_computation.158.clone.1 | convolution fusion | flops 162002944 | bytes 6638464 | tf_op jit(solution)/shard_map/while/body/eval_jaxpr/dot_general | solution.py:56
  443.1 2.5 fusion.141
  448.0 29.3 %fusion.139 = (f32[2048]{0:T(1024)S(1)}, f32[2048,384]{0,1:T(8,128)S(1)}) fusion(f32[]{:T(128)} %bitcast.298, f32[]{:T(128)} %bitcast.299, f32[]{:T(128)} %bitcast.300, f32[]{:T(128)} %bitcast.301, f32[]{:T(128)} %bitcast.302, f32[]{:T(128)} %bitcast.303, f32[]{:T(128)} %bitcast.304, f32[]{:T(128)} %bitcast.305, f32[]{:T(128)} %bitcast.306, ...), kind=kOutput, calls=%fused_computation.158.clone.1 | convolution fusion | flops 162002944 | bytes 6638464 | tf_op jit(solution)/shard_map/while/body/eval_jaxpr/dot_general | solution.py:56
  478.3 2.6 fusion.141
  483.2 29.3 %fusion.139 = (f32[2048]{0:T(1024)S(1)}, f32[2048,384]{0,1:T(8,128)S(1)}) fusion(f32[]{:T(128)} %bitcast.298, f32[]{:T(128)} %bitcast.299, f32[]{:T(128)} %bitcast.300, f32[]{:T(128)} %bitcast.301, f32[]{:T(128)} %bitcast.302, f32[]{:T(128)} %bitcast.303, f32[]{:T(128)} %bitcast.304, f32[]{:T(128)} %bitcast.305, f32[]{:T(128)} %bitcast.306, ...), kind=kOutput, calls=%fused_computation.158.clone.1 | convolution fusion | flops 162002944 | bytes 6638464 | tf_op jit(solution)/shard_map/while/body/eval_jaxpr/dot_general | solution.py:56
  518.4 29.3 %fusion.139 = (f32[2048]{0:T(1024)S(1)}, f32[2048,384]{0,1:T(8,128)S(1)}) fusion(f32[]{:T(128)} %bitcast.298, f32[]{:T(128)} %bitcast.299, f32[]{:T(128)} %bitcast.300, f32[]{:T(128)} %bitcast.301, f32[]{:T(128)} %bitcast.302, f32[]{:T(128)} %bitcast.303, f32[]{:T(128)} %bitcast.304, f32[]{:T(128)} %bitcast.305, f32[]{:T(128)} %bitcast.306, ...), kind=kOutput, calls=%fused_computation.158.clone.1 | convolution fusion | flops 162002944 | bytes 6638464 | tf_op jit(solution)/shard_map/while/body/eval_jaxpr/dot_general | solution.py:56
  548.7 2.5 fusion.141
  553.6 29.3 %fusion.139 = (f32[2048]{0:T(1024)S(1)}, f32[2048,384]{0,1:T(8,128)S(1)}) fusion(f32[]{:T(128)} %bitcast.298, f32[]{:T(128)} %bitcast.299, f32[]{:T(128)} %bitcast.300, f32[]{:T(128)} %bitcast.301, f32[]{:T(128)} %bitcast.302, f32[]{:T(128)} %bitcast.303, f32[]{:T(128)} %bitcast.304, f32[]{:T(128)} %bitcast.305, f32[]{:T(128)} %bitcast.306, ...), kind=kOutput, calls=%fused_computation.158.clone.1 | convolution fusion | flops 162002944 | bytes 6638464 | tf_op jit(solution)/shard_map/while/body/eval_jaxpr/dot_general | solution.py:56
  583.9 2.5 fusion.141
  588.7 29.3 %fusion.139 = (f32[2048]{0:T(1024)S(1)}, f32[2048,384]{0,1:T(8,128)S(1)}) fusion(f32[]{:T(128)} %bitcast.298, f32[]{:T(128)} %bitcast.299, f32[]{:T(128)} %bitcast.300, f32[]{:T(128)} %bitcast.301, f32[]{:T(128)} %bitcast.302, f32[]{:T(128)} %bitcast.303, f32[]{:T(128)} %bitcast.304, f32[]{:T(128)} %bitcast.305, f32[]{:T(128)} %bitcast.306, ...), kind=kOutput, calls=%fused_computation.158.clone.1 | convolution fusion | flops 162002944 | bytes 6638464 | tf_op jit(solution)/shard_map/while/body/eval_jaxpr/dot_general | solution.py:56
  619.0 2.6 fusion.141
  622.5 6.0 all-to-all-start.1
  629.1 4.3 all-to-all-done.1
  633.5 6.2 all-to-all-start
  639.7 3.6 copy.129
  643.3 3.0 copy.112
  646.3 7.4 all-to-all-start.2
  654.6 92.8 %all-to-all-done.2 = bf16[16,128,1024]{1,2,0:T(8,128)(2,1)} async-done(((bf16[16,128,1024]{1,2,0:T(8,128)(2,1)}), bf16[16,128,1024]{1,2,0:T(8,128)(2,1)}, u32[]{:S(2)}, u32[]{:S(2)}) %all-to-all-start.2) | async-done | bytes 4194336 | tf_op jit(solution)/shard_map/all_to_all | solution.py:136
  747.4 3.1 fusion.43
  753.3 19.7 %all_to_all.25 = bf16[16,20,1024]{2,1,0:T(8,128)(2,1)S(1)} all-to-all(bf16[16,20,1024]{2,1,0:T(8,128)(2,1)S(1)} %convolution_convert_fusion.1), channel_id=1, replica_groups=mesh['req'=16,'cuts'=16] {'req'}, dimensions={0} | all-to-all | bytes 1310720 | tf_op jit(solution)/shard_map/all_to_all | solution.py:175
  774.4 62.7 %all-gather.4.cloned.1.call-done = bf16[256,20,1024]{2,0,1:T(8,128)(2,1)} async-done(((bf16[16,20,1024]{2,0,1:T(8,128)(2,1)}), bf16[256,20,1024]{2,0,1:T(8,128)(2,1)}) %all-gather.4.cloned.1.call-update) | async-done | bytes 10485776 | tf_op jit(solution)/shard_map/all_gather | solution.py:177
  837.0 9.4 fusion.95
  846.4 18.0 %convolution_convert_fusion = bf16[256,20,1024]{2,0,1:T(8,128)(2,1)} fusion(f32[256,20,176]{0,2,1:T(8,128)} %fusion.95, bf16[256,20,1024]{2,0,1:T(8,128)(2,1)} %all-gather.4.cloned.1.call-done, bf16[1,1024,176]{1,2,0:T(8,128)(2,1)S(1)} %copy-done.7, bf16[1,1024,176]{1,2,0:T(8,128)(2,1)} %param.30), kind=kOutput, calls=%fused_computation.52 | convolution fusion | flops 3705241600 | bytes 25296896 | tf_op jit(solution)/shard_map/necf,edf->necd/dot_general | solution.py:96
  864.5 73.4 %reduce-scatter.2.cloned.1.call-done = bf16[16,20,1024]{2,0,1:T(8,128)(2,1)} async-done(((bf16[256,20,1024]{2,0,1:T(8,128)(2,1)}), bf16[16,20,1024]{2,0,1:T(8,128)(2,1)}) %reduce-scatter.2.cloned.1.call-update) | async-done | bytes 655376 | tf_op jit(solution)/shard_map/reduce_scatter | solution.py:180
  940.2 6.6 all-to-all-start.4
  946.9 3.3 convolution_bitcast_fusion
  950.1 9.3 all-to-all-done.4
  959.4 3.2 fusion.88
  (174 shorter events, 81.2 us)
Async XLA Ops:
  6.5 744.0 %copy-start = (bf16[1024,1024]{1,0:T(8,128)(2,1)S(1)}, bf16[1024,1024]{1,0:T(8,128)(2,1)}, u32[]{:S(2)}) copy-start(bf16[1024,1024]{1,0:T(8,128)(2,1)} %param.25) | copy-start | bytes 6291460
  6.5 52.4 %all-gather.6.cloned.1.call-start = ((), (), s32[]{:S(2)}) async-start(), calls=%async_computation.8 | async-start | bytes 4456448 | tf_op jit(solution)/shard_map/all_gather | solution.py:128
  622.5 11.0 %all-to-all-start.1 = ((bf16[16,128,16]{1,2,0:T(8,128)(2,1)}), bf16[16,128,16]{1,2,0:T(8,128)(2,1)S(1)}, u32[]{:S(2)}, u32[]{:S(2)}) async-start(bf16[16,128,16]{1,2,0:T(8,128)(2,1)} %copy_bitcast_fusion), calls=%async_computation.1 | async-start | bytes 131072 | tf_op jit(solution)/shard_map/all_to_all | solution.py:143
  633.5 12.9 %all-to-all-start = ((bf16[16,128,16]{1,2,0:T(8,128)(2,1)}), bf16[16,128,16]{1,2,0:T(8,128)(2,1)S(1)}, u32[]{:S(2)}, u32[]{:S(2)}) async-start(bf16[16,128,16]{1,2,0:T(8,128)(2,1)} %copy_bitcast_fusion.1), calls=%async_computation | async-start | bytes 131072 | tf_op jit(solution)/shard_map/all_to_all | solution.py:140
  646.3 7.6 copy-start.5
  646.3 7.6 copy-start.6
  646.3 101.1 %all-to-all-start.2 = ((bf16[16,128,1024]{1,2,0:T(8,128)(2,1)}), bf16[16,128,1024]{1,2,0:T(8,128)(2,1)}, u32[]{:S(2)}, u32[]{:S(2)}) async-start(bf16[16,128,1024]{1,2,0:T(8,128)(2,1)} %copy.112), calls=%async_computation.2 | async-start | bytes 8388608 | tf_op jit(solution)/shard_map/all_to_all | solution.py:136
  653.7 96.9 %copy-start.2 = (bf16[1,128,1024]{2,1,0:T(8,128)(2,1)S(1)}, bf16[1,128,1024]{2,1,0:T(8,128)(2,1)}, u32[]{:S(2)}) copy-start(bf16[1,128,1024]{2,1,0:T(8,128)(2,1)} %param.24) | copy-start | bytes 786436
  653.7 183.3 %all-gather.4.cloned.1.call-start = ((), (), s32[]{:S(2)}) async-start(), calls=%async_computation.6 | async-start | bytes 11141120 | tf_op jit(solution)/shard_map/all_gather | solution.py:177
  750.5 0.8 copy-start.4
  752.0 22.2 %copy-start.3 = (f32[128,2]{1,0:T(8,128)}, f32[128,2]{1,0:T(8,128)S(1)}, u32[]{:S(2)}) copy-start(f32[128,2]{1,0:T(8,128)S(1)} %get-tuple-element.164) | copy-start | bytes 3076
  753.3 83.7 %copy-start.1 = (bf16[1,1024,176]{1,2,0:T(8,128)(2,1)S(1)}, bf16[1,1024,176]{1,2,0:T(8,128)(2,1)}, u32[]{:S(2)}) copy-start(bf16[1,1024,176]{1,2,0:T(8,128)(2,1)} %param.29) | copy-start | bytes 1081348
  774.3 72.1 %copy-start.7 = (bf16[1,1024,176]{1,2,0:T(8,128)(2,1)S(1)}, bf16[1,1024,176]{1,2,0:T(8,128)(2,1)}, u32[]{:S(2)}) copy-start(bf16[1,1024,176]{1,2,0:T(8,128)(2,1)} %param.31) | copy-start | bytes 1081348
  774.3 163.6 %reduce-scatter.2.cloned.1.call-start = ((), (), s32[]{:S(2)}) async-start(), calls=%async_computation.7 | async-start | bytes 11141120 | tf_op jit(solution)/shard_map/reduce_scatter | solution.py:180
  940.2 19.2 %all-to-all-start.4 = ((bf16[16,20,1024]{2,1,0:T(8,128)(2,1)}), bf16[16,20,1024]{2,1,0:T(8,128)(2,1)S(1)}, u32[]{:S(2)}, u32[]{:S(2)}) async-start(bf16[16,20,1024]{2,1,0:T(8,128)(2,1)} %copy.120), calls=%async_computation.5 | async-start | bytes 1572864 | tf_op jit(solution)/shard_map/all_to_all | solution.py:188
Sparse Core Ops, SparseCore 0:
  9.1 49.7 all-gather.5
  774.4 62.5 all-gather.3
  864.6 73.2 reduce-scatter.1
where the time goes:
time: 976 us; the launch traced here: 969 us
  matrix products  545 us (56%)
  waiting for transfers between devices  274 us (28%)
  local copies, waits for them, and re-layouts  56 us (6%)
  other arithmetic  33 us (3%)
  starting transfers between devices  26.5 us (3%)
  blocking collectives  19.7 us (2%)
  between operations  14 us (1%)
    dot_general x16, matrix products, head_partial(): lax.dot_general(query_rows, key_rows, (((1,), (1,)), ((), ())), preferred...  469 us
    all_to_all x1, waiting for transfers between devices, per_device(): lax.all_to_all(shortened(block_out), 'cuts', split_axis=0, concat_axis=0,...  92.8 us
    reduce_scatter x1, waiting for transfers between devices, per_device(): lax.psum_scatter(expert_part(row_block, gate_weight, up_weight, down_weig...  73.4 us
    all_gather x1, waiting for transfers between devices, per_device(): gathered = lax.all_gather(arrived, 'cuts', axis=0, tiled=True)  62.7 us
    dot_general x16, matrix products, head_partial(): jnp.dot(weights.astype(jnp.bfloat16), value_rows, preferred_element_type=...  40.8 us
    all_gather x1, waiting for transfers between devices, per_device(): every_query = lax.all_gather(queries[0], 'cuts', axis=0, tiled=True)  31 us
    gather x32, local copies, waits for them, and re-layouts, head_partial(): masked = jnp.where(visible, scores + jnp.take(bias_table, bucket), -1e+30)  22.6 us
    all_to_all x1, blocking collectives, per_device(): lax.all_to_all(buffers, 'req', split_axis=0, concat_axis=0, tiled=True)  19.7 us
  transfers between devices with their start and end apart: 7, of which 6 were waited for; matrix products, arithmetic and copies ran while one was open for 3% of the time, Pallas kernels for 0%

commit v1 on v0

--- a/solution.py
+++ b/solution.py
@@ -4,8 +4,18 @@
 import numpy as np
 from jax import lax
 from jax.sharding import PartitionSpec as P
+from jax.lax import all_to_all, axis_size
 
 MAXDIST = 128
+
+
+def do_cards_all(base_x):
+    samples = []
+    for _ in range(axis_size("cuts")):
+        samples.append(base_x)
+    piece_now = jnp.stack(samples, axis=0)
+    block_now = all_to_all(piece_now, axis_name="cuts", concat_axis=0, split_axis=0)
+    return jnp.concatenate(block_now, axis=0)
 
 
 def shortened(value):
@@ -125,7 +135,7 @@
     query_total = q_rows * cut_count
     local_keys = jnp.concatenate([cache_keys[0], new_keys[0]], axis=0)
     local_values = jnp.concatenate([cache_values[0], new_values[0]], axis=0)
-    every_query = lax.all_gather(queries[0], "cuts", axis=0, tiled=True)
+    every_query = do_cards_all(queries[0])
     visible, bucket = block_masks(cut_index, length, cache_rows, q_rows, query_total, bucket_count)
     block_out, block_peak, block_total = block_partials(
         every_query, local_keys, local_values, relative_bias, visible, bucket

time: 976 us -> 1050 us (1.076)
  waiting for transfers between devices: 274 us -> 319 us
  local copies, waits for them, and re-layouts: 56 us -> 70.4 us
    all_to_all x0 -> x1, waiting for transfers between devices: none -> 76.4 us  [do_cards_all(): all_to_all(piece_now, axis_name='cuts', concat_axis=0, split_axis=0)]
    all_gather x1 -> x0, waiting for transfers between devices: 31 us -> none  [per_device(): every_query = lax.all_gather(queries[0], 'cuts', axis=0, tiled=True)]
    another operation x0 -> x3, local copies, waits for them, and re-layouts: none -> 11.3 us  [the longest x1 7.28 us: block_partials(): query_rows.reshape(query_rows.shape[0], head_count, head_dim)]
where the time goes in v1:
time: 1050 us; the launch traced here: 1040 us
  matrix products  550 us (52%)
  waiting for transfers between devices  319 us (30%)
  local copies, waits for them, and re-layouts  70.4 us (7%)
  starting transfers between devices  33.8 us (3%)
  other arithmetic  33 us (3%)
  blocking collectives  20 us (2%)
  between operations  14.4 us (1%)
    dot_general x16, matrix products, head_partial(): lax.dot_general(query_rows, key_rows, (((1,), (1,)), ((), ())), preferred...  473 us
    all_to_all x1, waiting for transfers between devices, per_device(): lax.all_to_all(shortened(block_out), 'cuts', split_axis=0, concat_axis=0,...  93 us
    all_to_all x1, waiting for transfers between devices, do_cards_all(): all_to_all(piece_now, axis_name='cuts', concat_axis=0, split_axis=0)  76.4 us
    reduce_scatter x1, waiting for transfers between devices, per_device(): lax.psum_scatter(expert_part(row_block, gate_weight, up_weight, down_weig...  73.4 us
    all_gather x1, waiting for transfers between devices, per_device(): gathered = lax.all_gather(arrived, 'cuts', axis=0, tiled=True)  62.5 us
    dot_general x16, matrix products, head_partial(): jnp.dot(weights.astype(jnp.bfloat16), value_rows, preferred_element_type=...  40.8 us
    gather x32, local copies, waits for them, and re-layouts, head_partial(): masked = jnp.where(visible, scores + jnp.take(bias_table, bucket), -1e+30)  22.8 us
  transfers between devices with their start and end apart: 7, of which 6 were waited for; matrix products, arithmetic and copies ran while one was open for 3% of the time, Pallas kernels for 0%

profile of v1, /device:TPU:97, one launch (start us, length us, event | category | flops | bytes accessed | tf_op | source)
XLA Modules:
  0.0 1041.5 jit_solution(15074535585873083652)
XLA Ops:
  7.8 2.8 stack.3
  10.6 8.1 all-to-all-start
  25.2 10.9 %convert_add_fusion = s32[2048,384]{0,1:T(8,128)} fusion(s32[384]{0:T(512)S(1)} %pad_add_fusion, s32[2048]{0:T(1024)S(1)} %iota_add_fusion), kind=kLoop, calls=%fused_computation.63 | loop fusion | flops 73924608 | bytes 3155456 | tf_op jit(solution)/shard_map/add | solution.py:48
  36.0 76.4 %all-to-all-done = bf16[16,128,1024]{1,2,0:T(8,128)(2,1)} async-done(((bf16[16,128,1024]{1,2,0:T(8,128)(2,1)}), bf16[16,128,1024]{1,2,0:T(8,128)(2,1)}, u32[]{:S(2)}, u32[]{:S(2)}) %all-to-all-start) | async-done | bytes 4194336 | tf_op jit(solution)/shard_map/all_to_all | solution.py:17
  112.4 6.8 copy.107
  119.2 7.3 reshape_reshape.3
  126.5 567.8 %while.15 = (s32[]{:T(128)}, bf16[16,2048,64]{1,2,0:T(8,128)(2,1)}, bf16[16,2048]{1,0:T(8,128)(2,1)S(1)}, bf16[16,2048]{1,0:T(8,128)(2,1)S(1)}, bf16[16,2048,64]...) while((s32[]{:T(128)}, bf16[16,2048,64]{1,2,0:T(8,128)(2,1)}, ...), condition=%wide.region_3.4_spmd.clone, body=%wide.region_0.3_spmd.clone.sunk | while | flops 270792704 | bytes 13345049 | solution.py:88
  128.6 29.6 %fusion.139 = (f32[2048]{0:T(1024)S(1)}, f32[2048,384]{0,1:T(8,128)S(1)}) fusion(f32[]{:T(128)} %bitcast.299, f32[]{:T(128)} %bitcast.300, f32[]{:T(128)} %bitcast.301, f32[]{:T(128)} %bitcast.302, f32[]{:T(128)} %bitcast.303, f32[]{:T(128)} %bitcast.304, f32[]{:T(128)} %bitcast.305, f32[]{:T(128)} %bitcast.306, f32[]{:T(128)} %bitcast.307, ...), kind=kOutput, calls=%fused_computation.158.clone.1 | convolution fusion | flops 162002944 | bytes 6638464 | tf_op jit(solution)/shard_map/while/body/eval_jaxpr/dot_general | solution.py:66
  164.1 29.6 %fusion.139 = (f32[2048]{0:T(1024)S(1)}, f32[2048,384]{0,1:T(8,128)S(1)}) fusion(f32[]{:T(128)} %bitcast.299, f32[]{:T(128)} %bitcast.300, f32[]{:T(128)} %bitcast.301, f32[]{:T(128)} %bitcast.302, f32[]{:T(128)} %bitcast.303, f32[]{:T(128)} %bitcast.304, f32[]{:T(128)} %bitcast.305, f32[]{:T(128)} %bitcast.306, f32[]{:T(128)} %bitcast.307, ...), kind=kOutput, calls=%fused_computation.158.clone.1 | convolution fusion | flops 162002944 | bytes 6638464 | tf_op jit(solution)/shard_map/while/body/eval_jaxpr/dot_general | solution.py:66
  194.7 2.6 fusion.141
  199.6 29.6 %fusion.139 = (f32[2048]{0:T(1024)S(1)}, f32[2048,384]{0,1:T(8,128)S(1)}) fusion(f32[]{:T(128)} %bitcast.299, f32[]{:T(128)} %bitcast.300, f32[]{:T(128)} %bitcast.301, f32[]{:T(128)} %bitcast.302, f32[]{:T(128)} %bitcast.303, f32[]{:T(128)} %bitcast.304, f32[]{:T(128)} %bitcast.305, f32[]{:T(128)} %bitcast.306, f32[]{:T(128)} %bitcast.307, ...), kind=kOutput, calls=%fused_computation.158.clone.1 | convolution fusion | flops 162002944 | bytes 6638464 | tf_op jit(solution)/shard_map/while/body/eval_jaxpr/dot_general | solution.py:66
  230.2 2.6 fusion.141
  235.1 29.6 %fusion.139 = (f32[2048]{0:T(1024)S(1)}, f32[2048,384]{0,1:T(8,128)S(1)}) fusion(f32[]{:T(128)} %bitcast.299, f32[]{:T(128)} %bitcast.300, f32[]{:T(128)} %bitcast.301, f32[]{:T(128)} %bitcast.302, f32[]{:T(128)} %bitcast.303, f32[]{:T(128)} %bitcast.304, f32[]{:T(128)} %bitcast.305, f32[]{:T(128)} %bitcast.306, f32[]{:T(128)} %bitcast.307, ...), kind=kOutput, calls=%fused_computation.158.clone.1 | convolution fusion | flops 162002944 | bytes 6638464 | tf_op jit(solution)/shard_map/while/body/eval_jaxpr/dot_general | solution.py:66
  265.7 2.6 fusion.141
  270.6 29.6 %fusion.139 = (f32[2048]{0:T(1024)S(1)}, f32[2048,384]{0,1:T(8,128)S(1)}) fusion(f32[]{:T(128)} %bitcast.299, f32[]{:T(128)} %bitcast.300, f32[]{:T(128)} %bitcast.301, f32[]{:T(128)} %bitcast.302, f32[]{:T(128)} %bitcast.303, f32[]{:T(128)} %bitcast.304, f32[]{:T(128)} %bitcast.305, f32[]{:T(128)} %bitcast.306, f32[]{:T(128)} %bitcast.307, ...), kind=kOutput, calls=%fused_computation.158.clone.1 | convolution fusion | flops 162002944 | bytes 6638464 | tf_op jit(solution)/shard_map/while/body/eval_jaxpr/dot_general | solution.py:66
  306.1 29.6 %fusion.139 = (f32[2048]{0:T(1024)S(1)}, f32[2048,384]{0,1:T(8,128)S(1)}) fusion(f32[]{:T(128)} %bitcast.299, f32[]{:T(128)} %bitcast.300, f32[]{:T(128)} %bitcast.301, f32[]{:T(128)} %bitcast.302, f32[]{:T(128)} %bitcast.303, f32[]{:T(128)} %bitcast.304, f32[]{:T(128)} %bitcast.305, f32[]{:T(128)} %bitcast.306, f32[]{:T(128)} %bitcast.307, ...), kind=kOutput, calls=%fused_computation.158.clone.1 | convolution fusion | flops 162002944 | bytes 6638464 | tf_op jit(solution)/shard_map/while/body/eval_jaxpr/dot_general | solution.py:66
  341.6 29.6 %fusion.139 = (f32[2048]{0:T(1024)S(1)}, f32[2048,384]{0,1:T(8,128)S(1)}) fusion(f32[]{:T(128)} %bitcast.299, f32[]{:T(128)} %bitcast.300, f32[]{:T(128)} %bitcast.301, f32[]{:T(128)} %bitcast.302, f32[]{:T(128)} %bitcast.303, f32[]{:T(128)} %bitcast.304, f32[]{:T(128)} %bitcast.305, f32[]{:T(128)} %bitcast.306, f32[]{:T(128)} %bitcast.307, ...), kind=kOutput, calls=%fused_computation.158.clone.1 | convolution fusion | flops 162002944 | bytes 6638464 | tf_op jit(solution)/shard_map/while/body/eval_jaxpr/dot_general | solution.py:66
  377.0 29.6 %fusion.139 = (f32[2048]{0:T(1024)S(1)}, f32[2048,384]{0,1:T(8,128)S(1)}) fusion(f32[]{:T(128)} %bitcast.299, f32[]{:T(128)} %bitcast.300, f32[]{:T(128)} %bitcast.301, f32[]{:T(128)} %bitcast.302, f32[]{:T(128)} %bitcast.303, f32[]{:T(128)} %bitcast.304, f32[]{:T(128)} %bitcast.305, f32[]{:T(128)} %bitcast.306, f32[]{:T(128)} %bitcast.307, ...), kind=kOutput, calls=%fused_computation.158.clone.1 | convolution fusion | flops 162002944 | bytes 6638464 | tf_op jit(solution)/shard_map/while/body/eval_jaxpr/dot_general | solution.py:66
  407.6 2.5 fusion.141
  412.5 29.6 %fusion.139 = (f32[2048]{0:T(1024)S(1)}, f32[2048,384]{0,1:T(8,128)S(1)}) fusion(f32[]{:T(128)} %bitcast.299, f32[]{:T(128)} %bitcast.300, f32[]{:T(128)} %bitcast.301, f32[]{:T(128)} %bitcast.302, f32[]{:T(128)} %bitcast.303, f32[]{:T(128)} %bitcast.304, f32[]{:T(128)} %bitcast.305, f32[]{:T(128)} %bitcast.306, f32[]{:T(128)} %bitcast.307, ...), kind=kOutput, calls=%fused_computation.158.clone.1 | convolution fusion | flops 162002944 | bytes 6638464 | tf_op jit(solution)/shard_map/while/body/eval_jaxpr/dot_general | solution.py:66
  448.0 29.6 %fusion.139 = (f32[2048]{0:T(1024)S(1)}, f32[2048,384]{0,1:T(8,128)S(1)}) fusion(f32[]{:T(128)} %bitcast.299, f32[]{:T(128)} %bitcast.300, f32[]{:T(128)} %bitcast.301, f32[]{:T(128)} %bitcast.302, f32[]{:T(128)} %bitcast.303, f32[]{:T(128)} %bitcast.304, f32[]{:T(128)} %bitcast.305, f32[]{:T(128)} %bitcast.306, f32[]{:T(128)} %bitcast.307, ...), kind=kOutput, calls=%fused_computation.158.clone.1 | convolution fusion | flops 162002944 | bytes 6638464 | tf_op jit(solution)/shard_map/while/body/eval_jaxpr/dot_general | solution.py:66
  478.6 2.6 fusion.141
  483.5 29.6 %fusion.139 = (f32[2048]{0:T(1024)S(1)}, f32[2048,384]{0,1:T(8,128)S(1)}) fusion(f32[]{:T(128)} %bitcast.299, f32[]{:T(128)} %bitcast.300, f32[]{:T(128)} %bitcast.301, f32[]{:T(128)} %bitcast.302, f32[]{:T(128)} %bitcast.303, f32[]{:T(128)} %bitcast.304, f32[]{:T(128)} %bitcast.305, f32[]{:T(128)} %bitcast.306, f32[]{:T(128)} %bitcast.307, ...), kind=kOutput, calls=%fused_computation.158.clone.1 | convolution fusion | flops 162002944 | bytes 6638464 | tf_op jit(solution)/shard_map/while/body/eval_jaxpr/dot_general | solution.py:66
  519.0 29.6 %fusion.139 = (f32[2048]{0:T(1024)S(1)}, f32[2048,384]{0,1:T(8,128)S(1)}) fusion(f32[]{:T(128)} %bitcast.299, f32[]{:T(128)} %bitcast.300, f32[]{:T(128)} %bitcast.301, f32[]{:T(128)} %bitcast.302, f32[]{:T(128)} %bitcast.303, f32[]{:T(128)} %bitcast.304, f32[]{:T(128)} %bitcast.305, f32[]{:T(128)} %bitcast.306, f32[]{:T(128)} %bitcast.307, ...), kind=kOutput, calls=%fused_computation.158.clone.1 | convolution fusion | flops 162002944 | bytes 6638464 | tf_op jit(solution)/shard_map/while/body/eval_jaxpr/dot_general | solution.py:66
  549.6 2.5 fusion.141
  554.5 29.6 %fusion.139 = (f32[2048]{0:T(1024)S(1)}, f32[2048,384]{0,1:T(8,128)S(1)}) fusion(f32[]{:T(128)} %bitcast.299, f32[]{:T(128)} %bitcast.300, f32[]{:T(128)} %bitcast.301, f32[]{:T(128)} %bitcast.302, f32[]{:T(128)} %bitcast.303, f32[]{:T(128)} %bitcast.304, f32[]{:T(128)} %bitcast.305, f32[]{:T(128)} %bitcast.306, f32[]{:T(128)} %bitcast.307, ...), kind=kOutput, calls=%fused_computation.158.clone.1 | convolution fusion | flops 162002944 | bytes 6638464 | tf_op jit(solution)/shard_map/while/body/eval_jaxpr/dot_general | solution.py:66
  585.1 2.5 fusion.141
  590.0 29.6 %fusion.139 = (f32[2048]{0:T(1024)S(1)}, f32[2048,384]{0,1:T(8,128)S(1)}) fusion(f32[]{:T(128)} %bitcast.299, f32[]{:T(128)} %bitcast.300, f32[]{:T(128)} %bitcast.301, f32[]{:T(128)} %bitcast.302, f32[]{:T(128)} %bitcast.303, f32[]{:T(128)} %bitcast.304, f32[]{:T(128)} %bitcast.305, f32[]{:T(128)} %bitcast.306, f32[]{:T(128)} %bitcast.307, ...), kind=kOutput, calls=%fused_computation.158.clone.1 | convolution fusion | flops 162002944 | bytes 6638464 | tf_op jit(solution)/shard_map/while/body/eval_jaxpr/dot_general | solution.py:66
  625.5 29.6 %fusion.139 = (f32[2048]{0:T(1024)S(1)}, f32[2048,384]{0,1:T(8,128)S(1)}) fusion(f32[]{:T(128)} %bitcast.299, f32[]{:T(128)} %bitcast.300, f32[]{:T(128)} %bitcast.301, f32[]{:T(128)} %bitcast.302, f32[]{:T(128)} %bitcast.303, f32[]{:T(128)} %bitcast.304, f32[]{:T(128)} %bitcast.305, f32[]{:T(128)} %bitcast.306, f32[]{:T(128)} %bitcast.307, ...), kind=kOutput, calls=%fused_computation.158.clone.1 | convolution fusion | flops 162002944 | bytes 6638464 | tf_op jit(solution)/shard_map/while/body/eval_jaxpr/dot_general | solution.py:66
  660.9 29.6 %fusion.139 = (f32[2048]{0:T(1024)S(1)}, f32[2048,384]{0,1:T(8,128)S(1)}) fusion(f32[]{:T(128)} %bitcast.299, f32[]{:T(128)} %bitcast.300, f32[]{:T(128)} %bitcast.301, f32[]{:T(128)} %bitcast.302, f32[]{:T(128)} %bitcast.303, f32[]{:T(128)} %bitcast.304, f32[]{:T(128)} %bitcast.305, f32[]{:T(128)} %bitcast.306, f32[]{:T(128)} %bitcast.307, ...), kind=kOutput, calls=%fused_computation.158.clone.1 | convolution fusion | flops 162002944 | bytes 6638464 | tf_op jit(solution)/shard_map/while/body/eval_jaxpr/dot_general | solution.py:66
  691.5 2.6 fusion.141
  695.0 5.3 all-to-all-start.2
  700.9 4.3 all-to-all-done.2
  705.2 6.3 all-to-all-start.1
  711.5 3.6 copy.134
  715.1 3.0 copy.117
  718.1 7.4 all-to-all-start.3
  726.2 93.0 %all-to-all-done.3 = bf16[16,128,1024]{1,2,0:T(8,128)(2,1)} async-done(((bf16[16,128,1024]{1,2,0:T(8,128)(2,1)}), bf16[16,128,1024]{1,2,0:T(8,128)(2,1)}, u32[]{:S(2)}, u32[]{:S(2)}) %all-to-all-start.3) | async-done | bytes 4194336 | tf_op jit(solution)/shard_map/all_to_all | solution.py:146
  819.2 3.1 fusion.43
  825.1 20.0 %all_to_all.30 = bf16[16,20,1024]{2,1,0:T(8,128)(2,1)S(1)} all-to-all(bf16[16,20,1024]{2,1,0:T(8,128)(2,1)S(1)} %convolution_convert_fusion.1), channel_id=1, replica_groups=mesh['req'=16,'cuts'=16] {'req'}, dimensions={0} | all-to-all | bytes 1310720 | tf_op jit(solution)/shard_map/all_to_all | solution.py:185
  846.6 62.5 %all-gather.2.cloned.1.call-done = bf16[256,20,1024]{2,0,1:T(8,128)(2,1)} async-done(((bf16[16,20,1024]{2,0,1:T(8,128)(2,1)}), bf16[256,20,1024]{2,0,1:T(8,128)(2,1)}) %all-gather.2.cloned.1.call-update) | async-done | bytes 10485776 | tf_op jit(solution)/shard_map/all_gather | solution.py:187
  909.1 9.4 fusion.95
  918.5 18.0 %convolution_convert_fusion = bf16[256,20,1024]{2,0,1:T(8,128)(2,1)} fusion(f32[256,20,176]{0,2,1:T(8,128)} %fusion.95, bf16[256,20,1024]{2,0,1:T(8,128)(2,1)} %all-gather.2.cloned.1.call-done, bf16[1,1024,176]{1,2,0:T(8,128)(2,1)S(1)} %copy-done.9, bf16[1,1024,176]{1,2,0:T(8,128)(2,1)} %param.30), kind=kOutput, calls=%fused_computation.52 | convolution fusion | flops 3705241600 | bytes 25296896 | tf_op jit(solution)/shard_map/necf,edf->necd/dot_general | solution.py:106
  936.5 73.4 %reduce-scatter.2.cloned.1.call-done = bf16[16,20,1024]{2,0,1:T(8,128)(2,1)} async-done(((bf16[256,20,1024]{2,0,1:T(8,128)(2,1)}), bf16[16,20,1024]{2,0,1:T(8,128)(2,1)}) %reduce-scatter.2.cloned.1.call-update) | async-done | bytes 655376 | tf_op jit(solution)/shard_map/reduce_scatter | solution.py:190
  1012.3 6.5 all-to-all-start.5
  1018.9 3.3 convolution_bitcast_fusion
  1022.1 9.3 all-to-all-done.5
  1031.4 3.2 fusion.88
  (180 shorter events, 88.9 us)
Async XLA Ops:
  6.5 815.8 %copy-start = (bf16[1024,1024]{1,0:T(8,128)(2,1)S(1)}, bf16[1024,1024]{1,0:T(8,128)(2,1)}, u32[]{:S(2)}) copy-start(bf16[1024,1024]{1,0:T(8,128)(2,1)} %param.25) | copy-start | bytes 6291460
  10.6 8.1 copy-start.3
  10.6 8.3 copy-start.1
  10.6 101.8 %all-to-all-start = ((bf16[16,128,1024]{1,2,0:T(8,128)(2,1)}), bf16[16,128,1024]{1,2,0:T(8,128)(2,1)}, u32[]{:S(2)}, u32[]{:S(2)}) async-start(bf16[16,128,1024]{1,2,0:T(8,128)(2,1)} %stack.3), calls=%async_computation | async-start | bytes 8388608 | tf_op jit(solution)/shard_map/all_to_all | solution.py:17
  695.0 10.3 all-to-all-start.2
  705.2 12.9 %all-to-all-start.1 = ((bf16[16,128,16]{1,2,0:T(8,128)(2,1)}), bf16[16,128,16]{1,2,0:T(8,128)(2,1)S(1)}, u32[]{:S(2)}, u32[]{:S(2)}) async-start(bf16[16,128,16]{1,2,0:T(8,128)(2,1)} %copy_bitcast_fusion.1), calls=%async_computation.1 | async-start | bytes 131072 | tf_op jit(solution)/shard_map/all_to_all | solution.py:150
  718.1 7.4 copy-start.7
  718.1 7.4 copy-start.8
  718.1 101.1 %all-to-all-start.3 = ((bf16[16,128,1024]{1,2,0:T(8,128)(2,1)}), bf16[16,128,1024]{1,2,0:T(8,128)(2,1)}, u32[]{:S(2)}, u32[]{:S(2)}) async-start(bf16[16,128,1024]{1,2,0:T(8,128)(2,1)} %copy.117), calls=%async_computation.3 | async-start | bytes 8388608 | tf_op jit(solution)/shard_map/all_to_all | solution.py:146
  725.5 96.9 %copy-start.4 = (bf16[1,128,1024]{2,1,0:T(8,128)(2,1)S(1)}, bf16[1,128,1024]{2,1,0:T(8,128)(2,1)}, u32[]{:S(2)}) copy-start(bf16[1,128,1024]{2,1,0:T(8,128)(2,1)} %param.24) | copy-start | bytes 786436
  725.5 183.6 %all-gather.2.cloned.1.call-start = ((), (), s32[]{:S(2)}) async-start(), calls=%async_computation.7 | async-start | bytes 11141120 | tf_op jit(solution)/shard_map/all_gather | solution.py:187
  822.3 0.8 copy-start.6
  823.8 22.5 %copy-start.5 = (f32[128,2]{1,0:T(8,128)}, f32[128,2]{1,0:T(8,128)S(1)}, u32[]{:S(2)}) copy-start(f32[128,2]{1,0:T(8,128)S(1)} %get-tuple-element.164) | copy-start | bytes 3076
  825.1 84.0 %copy-start.2 = (bf16[1,1024,176]{1,2,0:T(8,128)(2,1)S(1)}, bf16[1,1024,176]{1,2,0:T(8,128)(2,1)}, u32[]{:S(2)}) copy-start(bf16[1,1024,176]{1,2,0:T(8,128)(2,1)} %param.29) | copy-start | bytes 1081348
  846.3 72.1 %copy-start.9 = (bf16[1,1024,176]{1,2,0:T(8,128)(2,1)S(1)}, bf16[1,1024,176]{1,2,0:T(8,128)(2,1)}, u32[]{:S(2)}) copy-start(bf16[1,1024,176]{1,2,0:T(8,128)(2,1)} %param.31) | copy-start | bytes 1081348
  846.4 163.6 %reduce-scatter.2.cloned.1.call-start = ((), (), s32[]{:S(2)}) async-start(), calls=%async_computation.8 | async-start | bytes 11141120 | tf_op jit(solution)/shard_map/reduce_scatter | solution.py:190
  1012.3 19.1 %all-to-all-start.5 = ((bf16[16,20,1024]{2,1,0:T(8,128)(2,1)}), bf16[16,20,1024]{2,1,0:T(8,128)(2,1)S(1)}, u32[]{:S(2)}, u32[]{:S(2)}) async-start(bf16[16,20,1024]{2,1,0:T(8,128)(2,1)} %copy.125), calls=%async_computation.6 | async-start | bytes 1572864 | tf_op jit(solution)/shard_map/all_to_all | solution.py:198
Sparse Core Ops, SparseCore 0:
  846.5 62.5 all-gather.1
  936.6 73.2 reduce-scatter.1
